TPU v7x, 32 devices: a whole 2x2x4 slice. The times are simulated.
32 devices in a mesh: dp: 2 (over y), pipe: 4 (over z), tensor: 4 (over x, core).
Axes of the slice: x: 2, y: 2, z: 4, core: 2. Of those that a mesh axis runs over, the one named last changes fastest.
Arguments:
- kept_qkv: bfloat16 [2, 4, 3, 192, 6144], P('dp', 'pipe', None, None, 'tensor'), may hold values from -20 to 20
- held_qkv: bfloat16 [2, 4, 3, 192, 6144], P('dp', 'pipe', None, None, 'tensor'), may hold values from -20 to 20
- sent_grad: bfloat16 [2, 4, 2, 64, 6144], P('dp', 'pipe', None, 'tensor'), may hold values from -60 to 60
- order: int32 [2, 4], P('dp', 'pipe'), may hold values from 0 to 1
- offsets: int32 [2, 4, 2], P('dp'), may hold values from 0 to 128, as said below
Outputs:
- query_grad: bfloat16 [2, 4, 2, 64, 6144], P('dp', 'pipe', None, None, 'tensor')
- key_value_grad: bfloat16 [2, 4, 2, 2, 192, 6144], P('dp', 'pipe', None, None, None, 'tensor')
- bias_grad: float32 [4, 3, 6144], P('pipe', None, 'tensor')
Inputs may be any that keep to these rules, and one draw needn't show every extreme that they name: `offsets`: multiples of 64.
All inputs are finite; a program needn't handle non-finite values.
Results may differ from a plain program's by a relative error of at most 0.019.
Values may be sent and summed in bfloat16 or wider, within the bound.
No kernel may reach another device: no remote copies, remote signals or barrier semaphores. Data moves between devices by JAX's collectives and lax.ppermute only.
A program may use at most 64 MiB of HBM per device.

v0:
```python
import math
import jax
import jax.numpy as jnp
from jax import lax
from jax.sharding import PartitionSpec as P

HD = 128
MASK_FILL = -1e30


def from_behind(value, axis, steps):
    count = lax.axis_size(axis)
    pairs = [(source, (source + steps) % count) for source in range(count)]
    return lax.ppermute(value, axis, pairs)


def slice_backward(stash, grad_out, offset):
    key_count = stash.shape[1]
    row_count = grad_out.shape[0]
    feature_count = stash.shape[2]
    head_count = feature_count // HD
    score_scale = 1.0 / math.sqrt(HD)
    queries = lax.dynamic_slice_in_dim(stash[0], offset, row_count, 0).reshape(
        row_count, head_count, HD
    )
    key_rows = stash[1].reshape(key_count, head_count, HD)
    value_rows = stash[2].reshape(key_count, head_count, HD)
    out_grad = grad_out.reshape(row_count, head_count, HD)
    positions = offset + jnp.arange(row_count, dtype=jnp.int32)
    columns = jnp.arange(key_count, dtype=jnp.int32)
    visible = columns[None, :] <= positions[:, None]
    scores = (
        jnp.einsum("qhd,khd->hqk", queries, key_rows, preferred_element_type=jnp.float32)
        * score_scale
    )
    scores = jnp.where(visible[None], scores, MASK_FILL)
    row_max = jnp.max(scores, axis=-1, keepdims=True)
    expos = jnp.exp(scores - row_max)
    attention = expos / jnp.sum(expos, axis=-1, keepdims=True)
    attention_low = attention.astype(jnp.bfloat16)
    context = jnp.einsum(
        "hqk,khd->qhd", attention_low, value_rows, preferred_element_type=jnp.float32
    ).astype(jnp.bfloat16)
    delta = jnp.sum(out_grad.astype(jnp.float32) * context.astype(jnp.float32), axis=-1).T
    value_grad = jnp.einsum(
        "hqk,qhd->khd", attention_low, out_grad, preferred_element_type=jnp.float32
    ).astype(jnp.bfloat16)
    prob_grad = jnp.einsum("qhd,khd->hqk", out_grad, value_rows, preferred_element_type=jnp.float32)
    score_grad = (attention * (prob_grad - delta[:, :, None]) * score_scale).astype(jnp.bfloat16)
    query_grad = jnp.einsum(
        "hqk,khd->qhd", score_grad, key_rows, preferred_element_type=jnp.float32
    ).astype(jnp.bfloat16)
    key_grad = jnp.einsum(
        "hqk,qhd->khd", score_grad, queries, preferred_element_type=jnp.float32
    ).astype(jnp.bfloat16)
    both_grads = jnp.stack(
        [key_grad.reshape(key_count, feature_count), value_grad.reshape(key_count, feature_count)]
    )
    return (query_grad.reshape(row_count, feature_count), both_grads)


def body(kept_qkv, held_qkv, sent_grad, order, offsets):
    arrived = from_behind(sent_grad, "pipe", -1)
    regrouped = lax.all_to_all(arrived, "tensor", split_axis=4, concat_axis=3, tiled=True)
    kept_first = order[0, 0] == 0
    grad_kept = jnp.where(kept_first, regrouped[0, 0, 0], regrouped[0, 0, 1])
    grad_held = jnp.where(kept_first, regrouped[0, 0, 1], regrouped[0, 0, 0])
    section_index = lax.axis_index("pipe")
    section_count = lax.axis_size("pipe")
    half_way = section_count // 2
    section_offsets = lax.dynamic_index_in_dim(offsets[0], section_index, 0, keepdims=False)
    kept_q, kept_kv = slice_backward(kept_qkv[0, 0], grad_kept, section_offsets[0])
    fetched = from_behind(held_qkv[0, 0], "pipe", half_way)
    held_q, held_kv = slice_backward(fetched, grad_held, section_offsets[1])
    query_grad = jnp.stack([kept_q, held_q])
    key_value_grad = jnp.stack([kept_kv, held_kv])
    query_sums = jnp.sum(query_grad.astype(jnp.float32), axis=(0, 1))
    key_sums = jnp.sum(key_value_grad[:, 0].astype(jnp.float32), axis=(0, 1))
    value_sums = jnp.sum(key_value_grad[:, 1].astype(jnp.float32), axis=(0, 1))
    column_sums = jnp.stack([query_sums, key_sums, value_sums])
    bias_grad = lax.psum(column_sums, "dp")
    return (query_grad[None, None], key_value_grad[None, None], bias_grad[None])


def solution(mesh):
    return jax.shard_map(
        body,
        mesh=mesh,
        in_specs=(
            P("dp", "pipe", None, None, "tensor"),
            P("dp", "pipe", None, None, "tensor"),
            P("dp", "pipe", None, "tensor", None),
            P("dp", "pipe"),
            P("dp", None, None),
        ),
        out_specs=(
            P("dp", "pipe", None, None, "tensor"),
            P("dp", "pipe", None, None, None, "tensor"),
            P("pipe", None, "tensor"),
        ),
        check_vma=False,
    )
```

profile of v0, /device:TPU:8, one launch (start us, length us, event | category | flops | bytes accessed | tf_op | source)
XLA Modules:
  0.0 121.3 jit_solution(14244090203486681753)
XLA Ops:
  0.7 3.0 %collective-permute-start.1 = (bf16[3,192,1536]{2,1,0:T(8,128)(2,1)}, bf16[3,192,1536]{2,1,0:T(8,128)(2,1)}, u32[]{:S(2)}, u32[]{:S(2)}) collective-permute-start(bf16[3,192,1536]{2,1,0:T(8,128)(2,1)} %bitcast.67), channel_id=1, source_target_pairs={{0,8},{4,12},{8,0},{12,4},{1,9},{5,13},{9,1},{13,5},{2,10},{6,14},... | collective-permute-start | bytes 5308424 | tf_op jit(solution)/shard_map/ppermute | solution.py:14
  5.7 2.4 %fusion.54 = (bf16[1,1,1,192,1536]{4,3,2,1,0:T(8,128)(2,1)S(1)}, bf16[1,1,1,192,1536]{4,3,2,1,0:T(8,128)(2,1)}, bf16[1,1,1,192,1536]{4,3,2,1,0:T(8,128)(2,1)S(1)}) fusion(bf16[1,1,3,192,1536]{4,3,2,1,0:T(8,128)(2,1)} %param.5), kind=kLoop, calls=%fused_computation.86 | loop fusion | bytes 3538944 | tf_op jit(solution)/shard_map/slice | solution.py:23
  10.7 1.4 %fusion.7 = f32[12,64,192]{2,1,0:T(8,128)} fusion(bf16[192,12,128]{2,1,0:T(8,128)(2,1)S(1)} %reshape_squeeze.12, pred[64,192]{1,0:T(8,128)(4,1)S(1)} %iota_compare_fusion.1, bf16[64,12,128]{2,1,0:T(8,128)(2,1)S(1)} %reshape.94), kind=kOutput, calls=%fused_computation.22 | convolution fusion | flops 38043648 | bytes 1388544 | tf_op jit(solution)/shard_map/qhd,khd->hqk/dot_general | solution.py:33
  12.1 38.8 %collective-permute-done = bf16[1,1,2,16,6144]{4,3,2,1,0:T(8,128)(2,1)} collective-permute-done((bf16[1,1,2,16,6144]{4,3,2,1,0:T(8,128)(2,1)}, bf16[1,1,2,16,6144]{4,3,2,1,0:T(8,128)(2,1)}, u32[]{:S(2)}, u32[]{:S(2)}) %collective-permute-start) | collective-permute-done | bytes 393248 | tf_op jit(solution)/shard_map/ppermute | solution.py:14
  50.9 6.1 %copy.86 = bf16[1,1,2,16,6144]{3,2,1,0,4:T(2,128)(2,1)S(1)} copy(bf16[1,1,2,16,6144]{4,3,2,1,0:T(8,128)(2,1)} %collective-permute-done) | data formatting | bytes 786432 | tf_op jit(solution)/shard_map/ppermute | solution.py:14
  57.0 4.0 %reshape.96 = bf16[4,2,24576]{2,1,0:T(2,128)(2,1)} reshape(bf16[6144,1,1,2,16]{4,3,2,1,0:T(2,128)(2,1)S(1)} %bitcast.62) | data formatting | bytes 786432
  61.0 4.2 %all-to-all-start = ((bf16[4,2,24576]{2,1,0:T(2,128)(2,1)}), bf16[4,2,24576]{2,1,0:T(2,128)(2,1)}, u32[]{:S(2)}, u32[]{:S(2)}) async-start(bf16[4,2,24576]{2,1,0:T(2,128)(2,1)} %reshape.96), calls=%async_computation | async-start | bytes 786432 | tf_op jit(solution)/shard_map/all_to_all | solution.py:64
  66.6 2.2 %reshape_squeeze.13 = bf16[192,12,128]{2,1,0:T(8,128)(2,1)} reshape(bf16[1,1,1,192,1536]{4,3,2,1,0:T(8,128)(2,1)} %get-tuple-element.9) | data formatting | bytes 1179648 | tf_op jit(solution)/shard_map/reshape;squeeze | solution.py:27
  70.1 1.1 fusion.56
  71.2 1.5 %all-to-all-done = bf16[4,2,24576]{2,1,0:T(2,128)(2,1)} async-done(((bf16[4,2,24576]{2,1,0:T(2,128)(2,1)}), bf16[4,2,24576]{2,1,0:T(2,128)(2,1)}, u32[]{:S(2)}, u32[]{:S(2)}) %all-to-all-start) | async-done | bytes 393248 | tf_op jit(solution)/shard_map/all_to_all | solution.py:64
  72.7 3.5 %reshape.97 = bf16[6144,1,1,2,16]{4,3,2,1,0:T(2,128)(2,1)S(1)} reshape(bf16[4,2,24576]{2,1,0:T(2,128)(2,1)} %all-to-all-done) | data formatting | bytes 786432
  76.2 4.8 %copy.111 = bf16[1,1,2,16,4,1536]{5,4,3,2,1,0:T(4,128)(2,1)} copy(bf16[1,1,2,16,4,1536]{3,2,5,4,1,0:T(2,128)(2,1)S(1)} %bitcast.63) | data formatting | bytes 786432 | tf_op jit(solution)/shard_map/all_to_all | solution.py:64
  81.1 1.1 copy.88
  82.4 3.0 %fusion.27 = f32[64,12]{0,1:T(8,128)S(1)} fusion(bf16[192,12,128]{2,1,0:T(8,128)(2,1)S(1)} %copy-done.8, bf16[64,12,128]{2,1,0:T(8,128)(2,1)S(1)} %select_n.42, f32[12,64]{1,0:T(8,128)S(1)} %get-tuple-element.15, f32[12,64,192]{2,1,0:T(8,128)} %fusion.7), kind=kOutput, calls=%fused_computation.48 | convolution fusion | flops 38682816 | bytes 1382400 | tf_op jit(solution)/shard_map/hqk,khd->qhd/dot_general | solution.py:41
  88.0 3.1 %fusion.16 = bf16[192,12,128]{2,0,1:T(8,128)(2,1)S(1)} fusion(bf16[64,12,128]{2,1,0:T(8,128)(2,1)S(1)} %select_n.42, f32[12,64]{1,0:T(8,128)S(1)} %get-tuple-element.15, f32[12,64,192]{2,1,0:T(8,128)} %fusion.7), kind=kOutput, calls=%fused_computation.31 | convolution fusion | flops 38486976 | bytes 1379328 | tf_op jit(solution)/shard_map/hqk,qhd->khd/dot_general | solution.py:45
  93.8 1.5 %fusion.53 = (bf16[1,192,1536]{2,1,0:T(8,128)(2,1)S(1)}, bf16[1,192,1536]{2,1,0:T(8,128)(2,1)S(1)}, bf16[1,192,1536]{2,1,0:T(8,128)(2,1)S(1)}) fusion(bf16[3,192,1536]{2,1,0:T(8,128)(2,1)} %collective-permute-done.1), kind=kLoop, calls=%fused_computation.85 | loop fusion | bytes 3538944 | tf_op jit(solution)/shard_map/slice | solution.py:23
  95.4 1.3 %reshape_squeeze.15 = bf16[192,12,128]{2,1,0:T(8,128)(2,1)} reshape(bf16[1,192,1536]{2,1,0:T(8,128)(2,1)S(1)} %get-tuple-element.6) | data formatting | bytes 1179648 | tf_op jit(solution)/shard_map/reshape;squeeze | solution.py:27
  97.8 1.1 fusion.57
  98.9 2.5 %fusion.18 = bf16[192,12,128]{2,0,1:T(8,128)(2,1)} fusion(bf16[64,12,128]{2,1,0:T(8,128)(2,1)S(1)} %copy-done.10, f32[12,64]{1,0:T(8,128)S(1)} %get-tuple-element.17, f32[12,64,192]{2,1,0:T(8,128)S(1)} %fusion.10), kind=kOutput, calls=%fused_computation.33 | convolution fusion | flops 38486976 | bytes 1379328 | tf_op jit(solution)/shard_map/hqk,qhd->khd/dot_general | solution.py:45
  101.4 2.7 %fusion.28 = f32[64,12]{0,1:T(8,128)S(1)} fusion(bf16[192,12,128]{2,1,0:T(8,128)(2,1)} %reshape_squeeze.15, bf16[64,12,128]{2,1,0:T(8,128)(2,1)S(1)} %copy-done.10, f32[12,64]{1,0:T(8,128)S(1)} %get-tuple-element.17, f32[12,64,192]{2,1,0:T(8,128)S(1)} %fusion.10), kind=kOutput, calls=%fused_computation.49 | convolution fusion | flops 38682816 | bytes 1382400 | tf_op jit(solution)/shard_map/hqk,khd->qhd/dot_general | solution.py:41
  104.1 1.9 %fusion.13 = bf16[12,64,192]{2,1,0:T(8,128)(2,1)S(1)} fusion(bf16[192,12,128]{2,1,0:T(8,128)(2,1)} %reshape_squeeze.15, f32[12,64]{1,0:T(8,128)S(1)} %bitcast.68, f32[12,64,192]{2,1,0:T(8,128)} %get-tuple-element.18, f32[12,64]{1,0:T(8,128)S(1)} %get-tuple-element.17, bf16[64,12,128]{2,1,0:T(8,128)(2,1)S(1)} %copy-done.10), kind=kOutput, calls=%fused_computation.28 | convolution fusion | flops 38486016 | bytes 1677312 | tf_op jit(solution)/shard_map/qhd,khd->hqk/dot_general | solution.py:48
  106.0 1.0 fusion.30
  109.2 1.6 %fusion.2 = bf16[1,1,2,2,192,1536]{5,4,3,2,1,0:T(8,128)(2,1)} fusion(bf16[1,2,192,1536]{3,2,1,0:T(8,128)(2,1)S(1)} %get-tuple-element.20, bf16[1,2,192,1536]{3,2,1,0:T(8,128)(2,1)S(1)} %get-tuple-element.19), kind=kLoop, calls=%fused_computation.7 | loop fusion | flops 1179648 | bytes 4718592 | tf_op jit(solution)/shard_map/broadcast_in_dim | solution.py:82
  112.3 9.0 %psum.7 = f32[1,3,1536]{2,0,1:T(1,128)} all-reduce(f32[1,3,1536]{2,0,1:T(1,128)S(1)} %broadcast_in_dim.44), channel_id=1, replica_groups=mesh['dp'=2,'pipe'=4,'tensor'=4] {'dp'}, use_global_device_ids=true, to_apply=%region_9.10 | all-reduce | flops 4608 | bytes 36864 | tf_op jit(solution)/shard_map/psum | solution.py:81
  (66 shorter events, 12.9 us)
Async XLA Ops:
  0.6 3.1 %copy-start = (s32[1,4,2]{1,2,0:T(2,128)S(1)}, s32[1,4,2]{1,2,0:T(2,128)}, u32[]{:S(2)}) copy-start(s32[1,4,2]{1,2,0:T(2,128)} %param.9) | copy-start | bytes 100
  0.6 50.3 %collective-permute-start = (bf16[1,1,2,16,6144]{4,3,2,1,0:T(8,128)(2,1)}, bf16[1,1,2,16,6144]{4,3,2,1,0:T(8,128)(2,1)}, u32[]{:S(2)}, u32[]{:S(2)}) collective-permute-start(bf16[1,1,2,16,6144]{4,3,2,1,0:T(8,128)(2,1)} %param.7), channel_id=1, source_target_pairs={{0,12},{4,0},{8,4},{12,8},{1,13},{5,1},{9,5},{13,9},{2,14},{6,2},{... | collective-permute-start | bytes 1179656 | tf_op jit(solution)/shard_map/ppermute | solution.py:14
  0.7 93.1 %collective-permute-start.1 = (bf16[3,192,1536]{2,1,0:T(8,128)(2,1)}, bf16[3,192,1536]{2,1,0:T(8,128)(2,1)}, u32[]{:S(2)}, u32[]{:S(2)}) collective-permute-start(bf16[3,192,1536]{2,1,0:T(8,128)(2,1)} %bitcast.67), channel_id=1, source_target_pairs={{0,8},{4,12},{8,0},{12,4},{1,9},{5,13},{9,1},{13,5},{2,10},{6,14},... | collective-permute-start | bytes 5308424 | tf_op jit(solution)/shard_map/ppermute | solution.py:14
  9.9 2.2 %copy-start.1 = (bf16[192,12,128]{2,1,0:T(8,128)(2,1)}, bf16[192,12,128]{2,1,0:T(8,128)(2,1)S(1)}, u32[]{:S(2)}) copy-start(bf16[192,12,128]{2,1,0:T(8,128)(2,1)S(1)} %reshape_squeeze.12) | copy-start | bytes 1769476
  61.0 9.1 %copy-start.3 = (f32[12,64,192]{2,1,0:T(8,128)S(1)}, f32[12,64,192]{2,1,0:T(8,128)}, u32[]{:S(2)}) copy-start(f32[12,64,192]{2,1,0:T(8,128)} %fusion.7) | copy-start | bytes 1769476
  61.0 11.7 %all-to-all-start = ((bf16[4,2,24576]{2,1,0:T(2,128)(2,1)}), bf16[4,2,24576]{2,1,0:T(2,128)(2,1)}, u32[]{:S(2)}, u32[]{:S(2)}) async-start(bf16[4,2,24576]{2,1,0:T(2,128)(2,1)} %reshape.96), calls=%async_computation | async-start | bytes 786432 | tf_op jit(solution)/shard_map/all_to_all | solution.py:64
  81.1 1.3 %copy-start.8 = (bf16[192,12,128]{2,1,0:T(8,128)(2,1)S(1)}, bf16[192,12,128]{2,1,0:T(8,128)(2,1)}, u32[]{:S(2)}) copy-start(bf16[192,12,128]{2,1,0:T(8,128)(2,1)} %reshape_squeeze.13) | copy-start | bytes 1769476
  82.4 3.0 %copy-start.7 = (f32[12,64,192]{2,1,0:T(8,128)S(1)}, f32[12,64,192]{2,1,0:T(8,128)}, u32[]{:S(2)}) copy-start(f32[12,64,192]{2,1,0:T(8,128)} %get-tuple-element.16) | copy-start | bytes 1769476
  85.4 1.1 copy-start.2
  97.8 1.1 copy-start.10
  106.0 1.4 %copy-start.9 = (bf16[192,12,128]{2,0,1:T(8,128)(2,1)S(1)}, bf16[192,12,128]{2,0,1:T(8,128)(2,1)}, u32[]{:S(2)}) copy-start(bf16[192,12,128]{2,0,1:T(8,128)(2,1)} %fusion.18) | copy-start | bytes 1769476
  110.8 0.9 copy-start.6
  110.9 1.2 %copy-start.4 = (bf16[2,64,1536]{2,1,0:T(8,128)(2,1)S(1)}, bf16[2,64,1536]{2,1,0:T(8,128)(2,1)}, u32[]{:S(2)}) copy-start(bf16[2,64,1536]{2,1,0:T(8,128)(2,1)} %constant_dynamic-update-slice_fusion.1) | copy-start | bytes 1179652
  112.1 9.2 %copy-start.5 = (bf16[2,64,1536]{2,1,0:T(8,128)(2,1)}, bf16[2,64,1536]{2,1,0:T(8,128)(2,1)S(1)}, u32[]{:S(2)}) copy-start(bf16[2,64,1536]{2,1,0:T(8,128)(2,1)S(1)} %constant_dynamic-update-slice_fusion) | copy-start | bytes 1179652
where the time goes:
time: 122 us; the launch traced here: 121 us
  waiting for transfers between devices  40.4 us (33%)
  local copies, waits for them, and re-layouts  35.5 us (29%)
  matrix products  17.6 us (14%)
  blocking collectives  9.02 us (7%)
  starting transfers between devices  7.32 us (6%)
  other arithmetic  5.92 us (5%)
  between operations  5.53 us (5%)
    ppermute x2, waiting for transfers between devices, from_behind(): return lax.ppermute(value, axis, pairs)  38.8 us
    unnamed x25, local copies, waits for them, and re-layouts  9.33 us
    psum x1, blocking collectives, body(): bias_grad = lax.psum(column_sums, 'dp')  9.02 us
    ppermute x1, local copies, waits for them, and re-layouts, from_behind(): return lax.ppermute(value, axis, pairs)  6.09 us
    all_to_all x2, local copies, waits for them, and re-layouts, body(): lax.all_to_all(arrived, 'tensor', split_axis=4, concat_axis=3, tiled=True)  5.98 us
    dot_general x2, matrix products, slice_backward(): jnp.einsum('hqk,khd->qhd', attention_low, value_rows, preferred_element_t...  5.64 us
    dot_general x2, matrix products, slice_backward(): jnp.einsum('hqk,qhd->khd', attention_low, out_grad, preferred_element_typ...  5.59 us
    all_to_all x1, starting transfers between devices, body(): lax.all_to_all(arrived, 'tensor', split_axis=4, concat_axis=3, tiled=True)  4.24 us
  transfers between devices with their start and end apart: 3, of which 2 were waited for; matrix products, arithmetic and copies ran while one was open for 33% of the time, Pallas kernels for 0%

commit v1 on v0

--- a/solution.py
+++ b/solution.py
@@ -61,7 +61,12 @@
 
 def body(kept_qkv, held_qkv, sent_grad, order, offsets):
     arrived = from_behind(sent_grad, "pipe", -1)
-    regrouped = lax.all_to_all(arrived, "tensor", split_axis=4, concat_axis=3, tiled=True)
+    regrouped = jnp.concatenate(
+        lax.all_to_all(
+            jnp.stack(jnp.split(arrived, lax.axis_size("tensor"), axis=4)), "tensor", 0, 0
+        ),
+        axis=3,
+    )
     kept_first = order[0, 0] == 0
     grad_kept = jnp.where(kept_first, regrouped[0, 0, 0], regrouped[0, 0, 1])
     grad_held = jnp.where(kept_first, regrouped[0, 0, 1], regrouped[0, 0, 0])

time: 122 us -> 117 us (0.959)
  the two profiles are of different devices: /device:TPU:8 before, /device:TPU:0 now
where the time goes in v1:
time: 117 us
  waiting for transfers between devices  58.3 us (50%)
  matrix products  15.8 us (14%)
  local copies, waits for them, and re-layouts  12.8 us (11%)
  blocking collectives  8.89 us (8%)
  starting transfers between devices  8.56 us (7%)
  other arithmetic  6.69 us (6%)
  between operations  5.51 us (5%)
    ppermute x2, waiting for transfers between devices, from_behind(): return lax.ppermute(value, axis, pairs)  55.9 us
    psum x1, blocking collectives, body(): bias_grad = lax.psum(column_sums, 'dp')  8.89 us
    dot_general x2, matrix products, slice_backward(): jnp.einsum('hqk,khd->qhd', attention_low, value_rows, preferred_element_t...  5.45 us
    ppermute x2, starting transfers between devices, from_behind(): return lax.ppermute(value, axis, pairs)  5.1 us
    dot_general x2, matrix products, slice_backward(): jnp.einsum('hqk,qhd->khd', attention_low, out_grad, preferred_element_typ...  4.22 us
    dot_general x2, matrix products, slice_backward(): jnp.einsum('qhd,khd->hqk', out_grad, value_rows, preferred_element_type=j...  3.62 us
    all_to_all x1, starting transfers between devices, body(): lax.all_to_all(jnp.stack(jnp.split(arrived, lax.axis_size('tensor'), axis...  3.46 us
    slice x2, local copies, waits for them, and re-layouts, slice_backward(): stash[0]  3.07 us
  transfers between devices with their start and end apart: 3, of which 3 were waited for; matrix products, arithmetic and copies ran while one was open for 15% of the time, Pallas kernels for 0%

profile of v1, /device:TPU:0, one launch (start us, length us, event | category | flops | bytes accessed | tf_op | source)
XLA Modules:
  0.0 116.5 jit_solution(17221263920328095458)
XLA Ops:
  0.6 5.1 %collective-permute-start = (bf16[1,1,2,16,6144]{4,3,2,1,0:T(8,128)(2,1)}, bf16[1,1,2,16,6144]{4,3,2,1,0:T(8,128)(2,1)S(1)}, u32[]{:S(2)}, u32[]{:S(2)}) collective-permute-start(bf16[1,1,2,16,6144]{4,3,2,1,0:T(8,128)(2,1)} %param.7), channel_id=1, source_target_pairs={{0,12},{4,0},{8,4},{12,8},{1,13},{5,1},{9,5},{13,9},{2,14},{6,2},{... | collective-permute-start | bytes 1179656 | tf_op jit(solution)/shard_map/ppermute | solution.py:14
  5.8 0.5 fusion.55
  7.0 0.6 iota_add_fusion.1
  8.3 1.5 %fusion.54 = (bf16[1,1,1,192,1536]{4,3,2,1,0:T(8,128)(2,1)S(1)}, bf16[1,1,1,192,1536]{4,3,2,1,0:T(8,128)(2,1)S(1)}, bf16[1,1,1,192,1536]{4,3,2,1,0:T(8,128)(2,1)S(1)}) fusion(bf16[1,1,3,192,1536]{4,3,2,1,0:T(8,128)(2,1)} %param.5), kind=kLoop, calls=%fused_computation.91 | loop fusion | bytes 3538944 | tf_op jit(solution)/shard_map/slice | solution.py:23
  11.2 0.6 iota_add_fusion
  12.4 3.2 %collective-permute-done = bf16[1,1,2,16,6144]{4,3,2,1,0:T(8,128)(2,1)S(1)} collective-permute-done((bf16[1,1,2,16,6144]{4,3,2,1,0:T(8,128)(2,1)}, bf16[1,1,2,16,6144]{4,3,2,1,0:T(8,128)(2,1)S(1)}, u32[]{:S(2)}, u32[]{:S(2)}) %collective-permute-start) | collective-permute-done | bytes 393248 | tf_op jit(solution)/shard_map/ppermute | solution.py:14
  15.6 0.8 pad_maximum_fusion.1
  16.4 3.5 %all-to-all-start = ((bf16[4,1,1,2,16,1536]{5,4,3,2,1,0:T(8,128)(2,1)}), bf16[4,1,1,2,16,1536]{5,4,3,2,1,0:T(8,128)(2,1)S(1)}, u32[]{:S(2)}, u32[]{:S(2)}) async-start(bf16[4,1,1,2,16,1536]{5,4,3,2,1,0:T(8,128)(2,1)} %pad_maximum_fusion.1), calls=%async_computation | async-start | bytes 786432 | tf_op jit(solution)/shard_map/all_to_all | solution.py:65
  21.9 1.3 %reshape_squeeze.13 = bf16[192,12,128]{2,1,0:T(8,128)(2,1)} reshape(bf16[1,1,1,192,1536]{4,3,2,1,0:T(8,128)(2,1)S(1)} %get-tuple-element.9) | data formatting | bytes 1179648 | tf_op jit(solution)/shard_map/reshape;squeeze | solution.py:27
  23.8 1.1 fusion.56
  24.9 2.4 %all-to-all-done = bf16[4,1,1,2,16,1536]{5,4,3,2,1,0:T(8,128)(2,1)S(1)} async-done(((bf16[4,1,1,2,16,1536]{5,4,3,2,1,0:T(8,128)(2,1)}), bf16[4,1,1,2,16,1536]{5,4,3,2,1,0:T(8,128)(2,1)S(1)}, u32[]{:S(2)}, u32[]{:S(2)}) %all-to-all-start) | async-done | bytes 393248 | tf_op jit(solution)/shard_map/all_to_all | solution.py:65
  27.7 2.8 %fusion.27 = f32[64,12]{0,1:T(8,128)S(1)} fusion(bf16[192,12,128]{2,1,0:T(8,128)(2,1)} %reshape_squeeze.13, bf16[64,12,128]{2,1,0:T(8,128)(2,1)S(1)} %select_n.42, f32[12,64]{1,0:T(8,128)S(1)} %get-tuple-element.19, f32[12,64,192]{2,1,0:T(8,128)S(1)} %fusion.7), kind=kOutput, calls=%fused_computation.48 | convolution fusion | flops 38682816 | bytes 1382400 | tf_op jit(solution)/shard_map/hqk,khd->qhd/dot_general | solution.py:41
  30.5 1.7 %fusion.14 = bf16[12,64,192]{2,1,0:T(8,128)(2,1)S(1)} fusion(bf16[192,12,128]{2,1,0:T(8,128)(2,1)} %reshape_squeeze.13, f32[12,64]{1,0:T(8,128)S(1)} %bitcast.72, f32[12,64,192]{2,1,0:T(8,128)S(1)} %copy-done.3, f32[12,64]{1,0:T(8,128)S(1)} %get-tuple-element.19, bf16[64,12,128]{2,1,0:T(8,128)(2,1)} %copy-done.5), kind=kOutput, calls=%fused_computation.29 | convolution fusion | flops 38486016 | bytes 1677312 | tf_op jit(solution)/shard_map/qhd,khd->hqk/dot_general | solution.py:48
  34.2 1.7 %fusion.16 = bf16[192,12,128]{2,0,1:T(8,128)(2,1)S(1)} fusion(bf16[64,12,128]{2,1,0:T(8,128)(2,1)S(1)} %copy-done.6, f32[12,64]{1,0:T(8,128)S(1)} %get-tuple-element.19, f32[12,64,192]{2,1,0:T(8,128)S(1)} %fusion.7), kind=kOutput, calls=%fused_computation.31 | convolution fusion | flops 38486976 | bytes 1379328 | tf_op jit(solution)/shard_map/hqk,qhd->khd/dot_general | solution.py:45
  36.8 0.7 constant_dynamic-update-slice_fusion.1
  37.4 52.7 %collective-permute-done.1 = bf16[3,192,1536]{2,1,0:T(8,128)(2,1)} collective-permute-done((bf16[3,192,1536]{2,1,0:T(8,128)(2,1)}, bf16[3,192,1536]{2,1,0:T(8,128)(2,1)}, u32[]{:S(2)}, u32[]{:S(2)}) %collective-permute-start.1) | collective-permute-done | bytes 1769504 | tf_op jit(solution)/shard_map/ppermute | solution.py:14
  90.2 1.5 %fusion.53 = (bf16[1,192,1536]{2,1,0:T(8,128)(2,1)S(1)}, bf16[1,192,1536]{2,1,0:T(8,128)(2,1)S(1)}, bf16[1,192,1536]{2,1,0:T(8,128)(2,1)S(1)}) fusion(bf16[3,192,1536]{2,1,0:T(8,128)(2,1)} %collective-permute-done.1), kind=kLoop, calls=%fused_computation.90 | loop fusion | bytes 3538944 | tf_op jit(solution)/shard_map/slice | solution.py:23
  91.9 1.3 %reshape_squeeze.15 = bf16[192,12,128]{2,1,0:T(8,128)(2,1)} reshape(bf16[1,192,1536]{2,1,0:T(8,128)(2,1)S(1)} %get-tuple-element.6) | data formatting | bytes 1179648 | tf_op jit(solution)/shard_map/reshape;squeeze | solution.py:27
  94.1 1.1 fusion.57
  95.2 2.5 %fusion.18 = bf16[192,12,128]{2,0,1:T(8,128)(2,1)} fusion(bf16[64,12,128]{2,1,0:T(8,128)(2,1)S(1)} %select_n.46, f32[12,64]{1,0:T(8,128)S(1)} %get-tuple-element.21, f32[12,64,192]{2,1,0:T(8,128)S(1)} %fusion.10), kind=kOutput, calls=%fused_computation.33 | convolution fusion | flops 38486976 | bytes 1379328 | tf_op jit(solution)/shard_map/hqk,qhd->khd/dot_general | solution.py:45
  97.7 2.7 %fusion.28 = f32[64,12]{0,1:T(8,128)S(1)} fusion(bf16[192,12,128]{2,1,0:T(8,128)(2,1)} %reshape_squeeze.15, bf16[64,12,128]{2,1,0:T(8,128)(2,1)S(1)} %select_n.46, f32[12,64]{1,0:T(8,128)S(1)} %get-tuple-element.21, f32[12,64,192]{2,1,0:T(8,128)S(1)} %fusion.10), kind=kOutput, calls=%fused_computation.49 | convolution fusion | flops 38682816 | bytes 1382400 | tf_op jit(solution)/shard_map/hqk,khd->qhd/dot_general | solution.py:41
  100.4 1.9 %fusion.13 = bf16[12,64,192]{2,1,0:T(8,128)(2,1)S(1)} fusion(bf16[192,12,128]{2,1,0:T(8,128)(2,1)} %reshape_squeeze.15, f32[12,64]{1,0:T(8,128)S(1)} %bitcast.71, f32[12,64,192]{2,1,0:T(8,128)} %get-tuple-element.22, f32[12,64]{1,0:T(8,128)S(1)} %get-tuple-element.21, bf16[64,12,128]{2,1,0:T(8,128)(2,1)S(1)} %select_n.46), kind=kOutput, calls=%fused_computation.28 | convolution fusion | flops 38486016 | bytes 1677312 | tf_op jit(solution)/shard_map/qhd,khd->hqk/dot_general | solution.py:48
  105.5 1.6 %fusion.2 = bf16[1,1,2,2,192,1536]{5,4,3,2,1,0:T(8,128)(2,1)} fusion(bf16[1,2,192,1536]{3,2,1,0:T(8,128)(2,1)S(1)} %get-tuple-element.24, bf16[1,2,192,1536]{3,2,1,0:T(8,128)(2,1)S(1)} %get-tuple-element.23), kind=kLoop, calls=%fused_computation.7 | loop fusion | flops 1179648 | bytes 4718592 | tf_op jit(solution)/shard_map/broadcast_in_dim | solution.py:87
  107.6 8.9 %psum.7 = f32[1,3,1536]{2,0,1:T(1,128)} all-reduce(f32[1,3,1536]{2,0,1:T(1,128)S(1)} %broadcast_in_dim.44), channel_id=1, replica_groups=mesh['dp'=2,'pipe'=4,'tensor'=4] {'dp'}, use_global_device_ids=true, to_apply=%region_9.10 | all-reduce | flops 4608 | bytes 36864 | tf_op jit(solution)/shard_map/psum | solution.py:86
  (56 shorter events, 9.2 us)
Async XLA Ops:
  0.6 5.1 %copy-start = (s32[1,4,2]{1,2,0:T(2,128)S(1)}, s32[1,4,2]{1,2,0:T(2,128)}, u32[]{:S(2)}) copy-start(s32[1,4,2]{1,2,0:T(2,128)} %param.9) | copy-start | bytes 100
  0.6 14.9 %collective-permute-start = (bf16[1,1,2,16,6144]{4,3,2,1,0:T(8,128)(2,1)}, bf16[1,1,2,16,6144]{4,3,2,1,0:T(8,128)(2,1)S(1)}, u32[]{:S(2)}, u32[]{:S(2)}) collective-permute-start(bf16[1,1,2,16,6144]{4,3,2,1,0:T(8,128)(2,1)} %param.7), channel_id=1, source_target_pairs={{0,12},{4,0},{8,4},{12,8},{1,13},{5,1},{9,5},{13,9},{2,14},{6,2},{... | collective-permute-start | bytes 1179656 | tf_op jit(solution)/shard_map/ppermute | solution.py:14
  5.7 84.4 %collective-permute-start.1 = (bf16[3,192,1536]{2,1,0:T(8,128)(2,1)}, bf16[3,192,1536]{2,1,0:T(8,128)(2,1)}, u32[]{:S(2)}, u32[]{:S(2)}) collective-permute-start(bf16[3,192,1536]{2,1,0:T(8,128)(2,1)} %bitcast.70), channel_id=1, source_target_pairs={{0,8},{4,12},{8,0},{12,4},{1,9},{5,13},{9,1},{13,5},{2,10},{6,14},... | collective-permute-start | bytes 5308424 | tf_op jit(solution)/shard_map/ppermute | solution.py:14
  16.4 10.9 %all-to-all-start = ((bf16[4,1,1,2,16,1536]{5,4,3,2,1,0:T(8,128)(2,1)}), bf16[4,1,1,2,16,1536]{5,4,3,2,1,0:T(8,128)(2,1)S(1)}, u32[]{:S(2)}, u32[]{:S(2)}) async-start(bf16[4,1,1,2,16,1536]{5,4,3,2,1,0:T(8,128)(2,1)} %pad_maximum_fusion.1), calls=%async_computation | async-start | bytes 786432 | tf_op jit(solution)/shard_map/all_to_all | solution.py:65
  27.7 2.8 %copy-start.5 = (bf16[64,12,128]{2,1,0:T(8,128)(2,1)}, bf16[64,12,128]{2,1,0:T(8,128)(2,1)S(1)}, u32[]{:S(2)}) copy-start(bf16[64,12,128]{2,1,0:T(8,128)(2,1)S(1)} %select_n.42) | copy-start | bytes 589828
  27.7 2.8 %copy-start.3 = (f32[12,64,192]{2,1,0:T(8,128)S(1)}, f32[12,64,192]{2,1,0:T(8,128)}, u32[]{:S(2)}) copy-start(f32[12,64,192]{2,1,0:T(8,128)} %get-tuple-element.20) | copy-start | bytes 1769476
  33.3 1.0 copy-start.6
  103.0 1.1 copy-start.4
  105.5 1.9 %copy-start.1 = (bf16[2,64,1536]{2,1,0:T(8,128)(2,1)S(1)}, bf16[2,64,1536]{2,1,0:T(8,128)(2,1)}, u32[]{:S(2)}) copy-start(bf16[2,64,1536]{2,1,0:T(8,128)(2,1)} %constant_dynamic-update-slice_fusion.1) | copy-start | bytes 1179652
  107.5 9.1 %copy-start.2 = (bf16[2,64,1536]{2,1,0:T(8,128)(2,1)}, bf16[2,64,1536]{2,1,0:T(8,128)(2,1)S(1)}, u32[]{:S(2)}) copy-start(bf16[2,64,1536]{2,1,0:T(8,128)(2,1)S(1)} %constant_dynamic-update-slice_fusion) | copy-start | bytes 1179652
